TPU v7x, 256 devices: a whole 4x4x8 slice. The times are simulated.
256 devices in a mesh: ctx: 32 (over y, x, core), tp: 8 (over z).
Axes of the slice: x: 4, y: 4, z: 8, core: 2. Of those that a mesh axis runs over, the one named last changes fastest.
Arguments:
- queries: bfloat16 [8192, 4096], P('ctx', 'tp'), may hold values from -12 to 12, as said below
- key_rows: bfloat16 [8192, 1024], P('ctx', 'tp'), may hold values from -12 to 12, as said below
- value_rows: bfloat16 [8192, 1024], P('ctx', 'tp'), may hold values from -6 to 6
- segments: int32 [8192], replicated, may hold values from 0 to 63, never falling along the last dimension, each value on 1 to 4096 neighbouring positions
- owner_ids: int32 [8192, 1], P('ctx'), may hold values from 0 to 7; in each aligned block of 256 rows (0 to 255, 256 to 511, ...) at most 64 rows name the same one
- out_proj: bfloat16 [4096, 8192], P('tp'), may hold values from -0.09375 to 0.09375
- residual: bfloat16 [16384, 8192], P(('ctx', 'tp')), may hold values from -4 to 4
- norm_gain: float32 [8192], replicated, may hold values from 0.5 to 1.5
Outputs:
- hidden_out: bfloat16 [16384, 8192], P(('ctx', 'tp'))
- normed: bfloat16 [16384, 8192], P(('ctx', 'tp'))
Inputs may be any that keep to these rules, and one draw needn't show every extreme that they name: `segments`: never falling along the tokens; every document has 1 to 4096 tokens and one has exactly 4096. `owner_ids`: among the rows of one device's token block no owner is named more than 64 times; some owner is named exactly 64 times in some block. `queries`: Real-valued entries. `key_rows`: Real-valued entries.
All inputs are finite; a program needn't handle non-finite values.
Results may differ from a plain program's by a relative error of at most 0.01.
Values may be sent and summed in bfloat16 or wider, within the bound.
No kernel may reach another device: no remote copies, remote signals or barrier semaphores. Data moves between devices by JAX's collectives and lax.ppermute only.
A program may use at most 128 MiB of HBM per device.

v0:
```python
import math
import jax
import jax.numpy as jnp
from jax import lax
from jax.sharding import PartitionSpec as P

HEADS = 32
KV_HEADS = 8
HEAD_DIM = 128


def slot_sources(owners, row_rank, owner_here, slot_count):
    token_count = owners.shape[0]
    slot_numbers = jnp.arange(slot_count, dtype=jnp.int32)[:, None]
    matches = ((owners[None, :] == owner_here) & (row_rank[None, :] == slot_numbers)).astype(
        jnp.int32
    )
    token_index = jnp.sum(matches * jnp.arange(token_count, dtype=jnp.int32)[None, :], axis=1)
    filled = jnp.sum(matches, axis=1) > 0
    return (token_index, filled)


def on_device(queries, key_rows, value_rows, segments, owner_ids, out_proj, residual, norm_gain):
    rows_here = queries.shape[0]
    kv_local = key_rows.shape[1] // HEAD_DIM
    group_size = HEADS // KV_HEADS
    score_scale = 1.0 / math.sqrt(HEAD_DIM)
    my_start = lax.axis_index("ctx") * rows_here
    query_heads = queries.reshape(rows_here, kv_local, group_size, HEAD_DIM)
    query_pos = my_start + jnp.arange(rows_here, dtype=jnp.int32)
    query_seg = lax.dynamic_slice_in_dim(segments, my_start, rows_here, 0)
    start_state = (
        jnp.full((kv_local, group_size, rows_here), -1e30, jnp.float32),
        jnp.zeros((kv_local, group_size, rows_here), jnp.float32),
        jnp.zeros((kv_local, group_size, rows_here, HEAD_DIM), jnp.float32),
    )
    carried = start_state
    key_piece = lax.all_gather(key_rows, "ctx", axis=0, tiled=True)
    value_piece = lax.all_gather(value_rows, "ctx", axis=0, tiled=True)
    piece_rows = key_piece.shape[0]
    key_width = 512
    block_count = piece_rows // key_width
    key_blocks = key_piece.reshape(block_count, key_width, kv_local, HEAD_DIM)
    value_blocks = value_piece.reshape(block_count, key_width, kv_local, HEAD_DIM)

    def update(states, block_item):
        block_index, key_block, value_block = block_item
        key_start = block_index * key_width
        key_seg = lax.dynamic_slice_in_dim(segments, key_start, key_width, 0)
        key_pos = key_start + jnp.arange(key_width, dtype=jnp.int32)
        allowed = (query_seg[:, None] == key_seg[None, :]) & (
            key_pos[None, :] <= query_pos[:, None]
        )
        running_max, totals, weighted = states
        scores = (
            jnp.einsum("tkgd,skd->kgts", query_heads, key_block, preferred_element_type=jnp.float32)
            * score_scale
        )
        scores = jnp.where(allowed, scores, -1e30)
        new_max = jnp.maximum(running_max, jnp.max(scores, axis=-1))
        exponent = jnp.where(allowed, jnp.exp(scores - new_max[..., None]), 0.0)
        factor = jnp.exp(running_max - new_max)
        totals = totals * factor + jnp.sum(exponent, axis=-1)
        weighted = weighted * factor[..., None] + jnp.einsum(
            "kgts,skd->kgtd",
            exponent.astype(jnp.bfloat16),
            value_block,
            preferred_element_type=jnp.float32,
        )
        states = (new_max, totals, weighted)
        return (states, None)

    carried, _ = lax.scan(
        update, carried, (jnp.arange(block_count, dtype=jnp.int32), key_blocks, value_blocks)
    )
    running_max, totals, weighted = carried
    mixed_heads = weighted / totals[..., None]
    attended = jnp.transpose(mixed_heads, (2, 0, 1, 3)).reshape(rows_here, -1).astype(jnp.bfloat16)
    partial_rows = jnp.dot(attended, out_proj, preferred_element_type=jnp.float32).astype(
        jnp.bfloat16
    )
    slot_count = residual.shape[0]
    owner_count = lax.axis_size("tp")
    owner_here = lax.axis_index("tp")
    owners = owner_ids[:, 0]
    onehot = (owners[:, None] == jnp.arange(owner_count, dtype=jnp.int32)[None, :]).astype(
        jnp.int32
    )
    before = jnp.cumsum(onehot, axis=0) - onehot
    row_rank = jnp.sum(before * onehot, axis=1)
    summed = lax.psum(partial_rows.astype(jnp.float32).astype(jnp.bfloat16), "tp").astype(
        jnp.float32
    )
    token_index, filled = slot_sources(owners, row_rank, owner_here, slot_count)
    owned_rows = jnp.where(filled[:, None], jnp.take(summed, token_index, axis=0), 0.0)
    hidden_sum = residual.astype(jnp.float32) + owned_rows
    mean_square = jnp.mean(hidden_sum * hidden_sum, axis=-1, keepdims=True)
    normed = hidden_sum * lax.rsqrt(mean_square + 1e-05) * norm_gain
    return (hidden_sum.astype(jnp.bfloat16), normed.astype(jnp.bfloat16))


def solution(mesh):
    placed = (
        P("ctx", "tp"),
        P("ctx", "tp"),
        P("ctx", "tp"),
        P(),
        P("ctx", None),
        P("tp", None),
        P(("ctx", "tp"), None),
        P(),
    )
    return jax.shard_map(
        on_device,
        mesh=mesh,
        in_specs=placed,
        out_specs=(P(("ctx", "tp"), None), P(("ctx", "tp"), None)),
        check_vma=False,
    )
```

profile of v0, /device:TPU:1, one launch (start us, length us, event | category | flops | bytes accessed | tf_op | source)
XLA Modules:
  0.0 347.0 jit_solution(442870078505631397)
XLA Ops:
  7.2 0.7 all-gather.3.cloned.1.call-update
  7.9 0.7 all-gather.5.cloned.1.call-update
  8.7 1.1 copy.16
  10.0 0.8 dynamic_slice.17
  10.8 52.6 %all-gather.3.cloned.1.call-done = bf16[8192,128]{1,0:T(8,128)(2,1)} async-done(((bf16[256,128]{1,0:T(8,128)(2,1)}), bf16[8192,128]{1,0:T(8,128)(2,1)}) %all-gather.3.cloned.1.call-update) | async-done | bytes 2097168 | tf_op jit(solution)/shard_map/all_gather | solution.py:38
  63.3 50.6 %all-gather.5.cloned.1.call-done = bf16[8192,128]{1,0:T(8,128)(2,1)} async-done(((bf16[256,128]{1,0:T(8,128)(2,1)}), bf16[8192,128]{1,0:T(8,128)(2,1)}) %all-gather.5.cloned.1.call-update) | async-done | bytes 2097168 | tf_op jit(solution)/shard_map/all_gather | solution.py:39
  113.9 95.9 %while.15 = (s32[]{:T(128)}, f32[1,4,256]{2,1,0:T(4,128)S(1)}, f32[1,4,256]{2,1,0:T(4,128)S(1)}, f32[1,4,256,128]{3,2,1,0:T(8,128)S(1)}, s32[256]{0:T(256)S(1)},...) while((s32[]{:T(128)}, f32[1,4,256]{2,1,0:T(4,128)S(1)}, ...), condition=%wide.region_8.9_spmd.clone, body=%wide.region_5.8_spmd.clone.sunk | while | flops 276044544 | bytes 8468703 | solution.py:73
  115.1 0.8 dynamic_slice.39
  116.1 1.4 fusion.41
  117.5 1.8 fusion.44
  119.9 0.6 dynamic_slice.38
  121.1 0.8 dynamic_slice.39
  122.1 1.4 fusion.41
  123.5 1.8 fusion.44
  127.1 0.8 dynamic_slice.39
  128.1 1.4 fusion.41
  129.5 1.8 fusion.44
  131.9 0.6 dynamic_slice.38
  133.1 0.8 dynamic_slice.39
  134.1 1.4 fusion.41
  135.5 1.8 fusion.44
  139.1 0.8 dynamic_slice.39
  140.1 1.4 fusion.41
  141.5 1.8 fusion.44
  143.9 0.6 dynamic_slice.38
  145.1 0.8 dynamic_slice.39
  146.1 1.4 fusion.41
  147.5 1.8 fusion.44
  151.1 0.8 dynamic_slice.39
  152.1 1.4 fusion.41
  153.5 1.8 fusion.44
  157.1 0.8 dynamic_slice.39
  158.1 1.4 fusion.41
  159.5 1.8 fusion.44
  163.1 0.8 dynamic_slice.39
  164.1 1.4 fusion.41
  165.5 1.8 fusion.44
  169.1 0.8 dynamic_slice.39
  170.1 1.4 fusion.41
  171.5 1.8 fusion.44
  175.1 0.8 dynamic_slice.39
  176.1 1.4 fusion.41
  177.5 1.8 fusion.44
  181.1 0.8 dynamic_slice.39
  182.1 1.4 fusion.41
  183.5 1.8 fusion.44
  187.1 0.8 dynamic_slice.39
  188.1 1.4 fusion.41
  189.5 1.8 fusion.44
  193.1 0.8 dynamic_slice.39
  194.1 1.4 fusion.41
  195.5 1.8 fusion.44
  199.1 0.8 dynamic_slice.39
  200.1 1.4 fusion.41
  201.5 1.8 fusion.44
  205.1 0.8 dynamic_slice.39
  206.0 1.4 fusion.41
  207.5 1.8 fusion.44
  210.1 7.7 %convolution_convert_fusion = bf16[256,8192]{1,0:T(8,128)(2,1)} fusion(bf16[256,512]{0,1:T(8,128)(2,1)S(1)} %bitcast.97, bf16[512,8192]{1,0:T(8,128)(2,1)} %param.15), kind=kOutput, calls=%fused_computation.35 | convolution fusion | flops 2149580800 | bytes 12845056 | tf_op jit(solution)/shard_map/dot_general | solution.py:79
  217.8 0.7 copy-done.2
  219.6 106.2 %all-reduce.2.cloned.1.call-done = bf16[256,8192]{1,0:T(8,128)(2,1)} async-done(((bf16[256,8192]{1,0:T(8,128)(2,1)}), bf16[256,8192]{1,0:T(8,128)(2,1)}) %all-reduce.2.cloned.1.call-update) | async-done | bytes 4194320 | tf_op jit(solution)/shard_map/psum | solution.py:91
  325.7 6.4 %convert_element_type.47 = f32[256,8192]{1,0:T(8,128)} convert(bf16[256,8192]{1,0:T(8,128)(2,1)} %all-reduce.2.cloned.1.call-done) | non-fusion elementwise | flops 2097152 | bytes 12582912 | tf_op jit(solution)/shard_map/convert_element_type | solution.py:91
  332.1 5.7 %gather_fusion = f32[64,8192]{1,0:T(8,128)S(1)} fusion(f32[256,8192]{1,0:T(8,128)} %convert_element_type.47, s32[1024]{0:T(1024)S(1)} %pad_clamp_fusion), kind=kCustom, calls=%fused_computation | custom fusion | bytes 4194560 | tf_op jit(solution)/shard_map/jit(_take)/gather | solution.py:95
  338.6 1.9 multiply_convert_fusion
  (154 shorter events, 22.5 us)
Async XLA Ops:
  7.2 56.2 %all-gather.3.cloned.1.call-start = ((), (), s32[]{:S(2)}) async-start(), calls=%async_computation | async-start | bytes 2162688 | tf_op jit(solution)/shard_map/all_gather | solution.py:38
  7.9 106.0 %all-gather.5.cloned.1.call-start = ((), (), s32[]{:S(2)}) async-start(), calls=%async_computation.1 | async-start | bytes 2162688 | tf_op jit(solution)/shard_map/all_gather | solution.py:39
  8.6 317.1 %all-reduce.2.cloned.1.call-start = ((), (), s32[]{:S(2)}) async-start(), calls=%async_computation.2 | async-start | bytes 8388608 | tf_op jit(solution)/shard_map/psum | solution.py:91
  217.8 0.7 copy-start.2
  332.1 5.7 %copy-start = (bf16[64,8192]{1,0:T(8,128)(2,1)S(1)}, bf16[64,8192]{1,0:T(8,128)(2,1)}, u32[]{:S(2)}) copy-start(bf16[64,8192]{1,0:T(8,128)(2,1)} %param.16) | copy-start | bytes 3145732
  337.8 0.8 copy-start.1
Sparse Core Ops, SparseCore 0:
  10.5 52.7 all-gather.2
  65.9 47.9 all-gather.4
  217.9 107.7 all-reduce.1
where the time goes:
time: 349 us; the launch traced here: 347 us
  waiting for transfers between devices  211 us (60%)
  matrix products  58.6 us (17%)
  local copies, waits for them, and re-layouts  30.7 us (9%)
  other arithmetic  22.1 us (6%)
  between operations  13.9 us (4%)
  loops' own time  10.9 us (3%)
    psum x1, waiting for transfers between devices, on_device(): lax.psum(partial_rows.astype(jnp.float32).astype(jnp.bfloat16), 'tp')  106 us
    all_gather x1, waiting for transfers between devices, on_device(): key_piece = lax.all_gather(key_rows, 'ctx', axis=0, tiled=True)  52.6 us
    all_gather x1, waiting for transfers between devices, on_device(): value_piece = lax.all_gather(value_rows, 'ctx', axis=0, tiled=True)  50.6 us
    dot_general x16, matrix products, update(): jnp.einsum('kgts,skd->kgtd', exponent.astype(jnp.bfloat16), value_block,...  28.7 us
    dot_general x16, matrix products, update(): jnp.einsum('tkgd,skd->kgts', query_heads, key_block, preferred_element_ty...  22.3 us
    dynamic_slice x16, local copies, waits for them, and re-layouts, update(): key_seg = lax.dynamic_slice_in_dim(segments, key_start, key_width, 0)  12.2 us
    another operation x1, loops' own time, on_device(): lax.scan(update, carried, (jnp.arange(block_count, dtype=jnp.int32), key_...  10.9 us
    dynamic_slice x16, local copies, waits for them, and re-layouts, on_device(): lax.scan(update, carried, (jnp.arange(block_count, dtype=jnp.int32), key_...  9.51 us
  transfers between devices with their start and end apart: 3, of which 3 were waited for; matrix products, arithmetic and copies ran while one was open for 1% of the time, Pallas kernels for 0%

commit v1 on v0

--- a/solution.py
+++ b/solution.py
@@ -36,7 +36,9 @@
     )
     carried = start_state
     key_piece = lax.all_gather(key_rows, "ctx", axis=0, tiled=True)
-    value_piece = lax.all_gather(value_rows, "ctx", axis=0, tiled=True)
+    value_piece = jnp.concatenate(
+        lax.all_to_all(jnp.stack([value_rows] * lax.axis_size("ctx")), "ctx", 0, 0), axis=0
+    )
     piece_rows = key_piece.shape[0]
     key_width = 512
     block_count = piece_rows // key_width

time: 349 us -> 309 us (0.89)
  waiting for transfers between devices: 211 us -> 160 us
  starting transfers between devices: 0.11 us -> 8.84 us
    all_gather x1 -> x0, waiting for transfers between devices: 50.6 us -> none  [on_device(): value_piece = lax.all_gather(value_rows, 'ctx', axis=0, tiled=True)]
    all_to_all x0 -> x1, waiting for transfers between devices: none -> 28.3 us  [on_device(): lax.all_to_all(jnp.stack([value_rows] * lax.axis_size('ctx')), 'ctx', 0, 0)]
    all_gather x1, waiting for transfers between devices: 52.6 us -> 25 us  [on_device(): key_piece = lax.all_gather(key_rows, 'ctx', axis=0, tiled=True)]
    all_to_all x0 -> x1, starting transfers between devices: none -> 8.76 us  [on_device(): lax.all_to_all(jnp.stack([value_rows] * lax.axis_size('ctx')), 'ctx', 0, 0)]
  transfers between devices with their start and end apart: 3 -> 3, of which waited for: 3 -> 3; matrix products, arithmetic and copies ran while one was open for 1% -> 2% of each run, Pallas kernels for 0% -> 0%
where the time goes in v1:
time: 309 us; the launch traced here: 307 us
  waiting for transfers between devices  160 us (52%)
  matrix products  58.4 us (19%)
  local copies, waits for them, and re-layouts  32.4 us (10%)
  other arithmetic  22.1 us (7%)
  between operations  14.2 us (5%)
  loops' own time  10.9 us (4%)
  starting transfers between devices  8.84 us (3%)
    psum x1, waiting for transfers between devices, on_device(): lax.psum(partial_rows.astype(jnp.float32).astype(jnp.bfloat16), 'tp')  106 us
    dot_general x16, matrix products, update(): jnp.einsum('kgts,skd->kgtd', exponent.astype(jnp.bfloat16), value_block,...  28.4 us
    all_to_all x1, waiting for transfers between devices, on_device(): lax.all_to_all(jnp.stack([value_rows] * lax.axis_size('ctx')), 'ctx', 0, 0)  28.3 us
    all_gather x1, waiting for transfers between devices, on_device(): key_piece = lax.all_gather(key_rows, 'ctx', axis=0, tiled=True)  25 us
    dot_general x16, matrix products, update(): jnp.einsum('tkgd,skd->kgts', query_heads, key_block, preferred_element_ty...  22.2 us
    dynamic_slice x16, local copies, waits for them, and re-layouts, update(): key_seg = lax.dynamic_slice_in_dim(segments, key_start, key_width, 0)  12.2 us
    another operation x1, loops' own time, on_device(): lax.scan(update, carried, (jnp.arange(block_count, dtype=jnp.int32), key_...  10.9 us
    dynamic_slice x16, local copies, waits for them, and re-layouts, on_device(): lax.scan(update, carried, (jnp.arange(block_count, dtype=jnp.int32), key_...  9.51 us
  transfers between devices with their start and end apart: 3, of which 3 were waited for; matrix products, arithmetic and copies ran while one was open for 2% of the time, Pallas kernels for 0%

profile of v1, /device:TPU:1, one launch (start us, length us, event | category | flops | bytes accessed | tf_op | source)
XLA Modules:
  0.0 307.0 jit_solution(11400248227723913571)
XLA Ops:
  7.2 0.7 all-gather.2.cloned.1.call-update
  7.9 2.6 stack.2
  10.5 8.8 %all-to-all-start = ((bf16[32,256,128]{2,1,0:T(8,128)(2,1)}), bf16[32,256,128]{2,1,0:T(8,128)(2,1)}, u32[]{:S(2)}, u32[]{:S(2)}) async-start(bf16[32,256,128]{2,1,0:T(8,128)(2,1)} %stack.2), calls=%async_computation | async-start | bytes 4194304 | tf_op jit(solution)/shard_map/all_to_all | solution.py:40
  19.7 0.8 dynamic_slice.17
  20.5 28.3 %all-to-all-done = bf16[32,256,128]{2,1,0:T(8,128)(2,1)} async-done(((bf16[32,256,128]{2,1,0:T(8,128)(2,1)}), bf16[32,256,128]{2,1,0:T(8,128)(2,1)}, u32[]{:S(2)}, u32[]{:S(2)}) %all-to-all-start) | async-done | bytes 2097184 | tf_op jit(solution)/shard_map/all_to_all | solution.py:40
  48.8 25.0 %all-gather.2.cloned.1.call-done = bf16[8192,128]{1,0:T(8,128)(2,1)} async-done(((bf16[256,128]{1,0:T(8,128)(2,1)}), bf16[8192,128]{1,0:T(8,128)(2,1)}) %all-gather.2.cloned.1.call-update) | async-done | bytes 2097168 | tf_op jit(solution)/shard_map/all_gather | solution.py:38
  73.8 95.6 %while.15 = (s32[]{:T(128)}, f32[1,4,256]{2,1,0:T(4,128)S(1)}, f32[1,4,256]{2,1,0:T(4,128)S(1)}, f32[1,4,256,128]{3,2,1,0:T(8,128)S(1)}, s32[256]{0:T(256)S(1)},...) while((s32[]{:T(128)}, f32[1,4,256]{2,1,0:T(4,128)S(1)}, ...), condition=%wide.region_8.9_spmd.clone, body=%wide.region_5.8_spmd.clone.sunk | while | flops 276044544 | bytes 8468703 | solution.py:75
  75.0 0.8 dynamic_slice.39
  76.0 1.4 fusion.41
  77.4 1.8 fusion.44
  81.0 0.8 dynamic_slice.39
  82.0 1.4 fusion.41
  83.4 1.8 fusion.44
  87.0 0.8 dynamic_slice.39
  88.0 1.4 fusion.41
  89.4 1.8 fusion.44
  91.7 0.6 dynamic_slice.38
  93.0 0.8 dynamic_slice.39
  93.9 1.4 fusion.41
  95.4 1.8 fusion.44
  98.9 0.8 dynamic_slice.39
  99.9 1.4 fusion.41
  101.3 1.8 fusion.44
  104.9 0.8 dynamic_slice.39
  105.9 1.4 fusion.41
  107.3 1.8 fusion.44
  109.7 0.6 dynamic_slice.38
  110.9 0.8 dynamic_slice.39
  111.9 1.4 fusion.41
  113.3 1.8 fusion.44
  115.7 0.6 dynamic_slice.38
  116.9 0.8 dynamic_slice.39
  117.9 1.4 fusion.41
  119.3 1.8 fusion.44
  122.9 0.8 dynamic_slice.39
  123.8 1.4 fusion.41
  125.3 1.8 fusion.44
  128.8 0.8 dynamic_slice.39
  129.8 1.4 fusion.41
  131.2 1.8 fusion.44
  134.8 0.8 dynamic_slice.39
  135.8 1.4 fusion.41
  137.2 1.8 fusion.44
  140.8 0.8 dynamic_slice.39
  141.8 1.4 fusion.41
  143.2 1.8 fusion.44
  146.8 0.8 dynamic_slice.39
  147.8 1.4 fusion.41
  149.2 1.8 fusion.44
  152.8 0.8 dynamic_slice.39
  153.7 1.4 fusion.41
  155.2 1.8 fusion.44
  158.7 0.8 dynamic_slice.39
  159.7 1.4 fusion.41
  161.1 1.8 fusion.44
  164.7 0.8 dynamic_slice.39
  165.7 1.4 fusion.41
  167.1 1.8 fusion.44
  169.7 7.7 %convolution_convert_fusion = bf16[256,8192]{1,0:T(8,128)(2,1)} fusion(bf16[256,512]{0,1:T(8,128)(2,1)S(1)} %bitcast.97, bf16[512,8192]{1,0:T(8,128)(2,1)} %param.15), kind=kOutput, calls=%fused_computation.35 | convolution fusion | flops 2149580800 | bytes 12845056 | tf_op jit(solution)/shard_map/dot_general | solution.py:81
  177.4 0.7 copy-done.3
  179.2 106.2 %all-reduce.2.cloned.1.call-done = bf16[256,8192]{1,0:T(8,128)(2,1)} async-done(((bf16[256,8192]{1,0:T(8,128)(2,1)}), bf16[256,8192]{1,0:T(8,128)(2,1)}) %all-reduce.2.cloned.1.call-update) | async-done | bytes 4194320 | tf_op jit(solution)/shard_map/psum | solution.py:93
  285.4 6.4 %convert_element_type.47 = f32[256,8192]{1,0:T(8,128)} convert(bf16[256,8192]{1,0:T(8,128)(2,1)} %all-reduce.2.cloned.1.call-done) | non-fusion elementwise | flops 2097152 | bytes 12582912 | tf_op jit(solution)/shard_map/convert_element_type | solution.py:93
  291.8 5.7 %gather_fusion = f32[64,8192]{1,0:T(8,128)S(1)} fusion(f32[256,8192]{1,0:T(8,128)} %convert_element_type.47, s32[1024]{0:T(1024)S(1)} %pad_clamp_fusion), kind=kCustom, calls=%fused_computation | custom fusion | bytes 4194560 | tf_op jit(solution)/shard_map/jit(_take)/gather | solution.py:97
  298.2 1.9 multiply_convert_fusion
  (156 shorter events, 22.6 us)
Async XLA Ops:
  7.2 66.6 %all-gather.2.cloned.1.call-start = ((), (), s32[]{:S(2)}) async-start(), calls=%async_computation.1 | async-start | bytes 2162688 | tf_op jit(solution)/shard_map/all_gather | solution.py:38
  10.5 8.9 %copy-start.1 = (bf16[256,512]{1,0:T(8,128)(2,1)S(1)}, bf16[256,512]{1,0:T(8,128)(2,1)}, u32[]{:S(2)}) copy-start(bf16[256,512]{1,0:T(8,128)(2,1)} %param.10) | copy-start | bytes 786436
  10.5 38.3 %all-to-all-start = ((bf16[32,256,128]{2,1,0:T(8,128)(2,1)}), bf16[32,256,128]{2,1,0:T(8,128)(2,1)}, u32[]{:S(2)}, u32[]{:S(2)}) async-start(bf16[32,256,128]{2,1,0:T(8,128)(2,1)} %stack.2), calls=%async_computation | async-start | bytes 4194304 | tf_op jit(solution)/shard_map/all_to_all | solution.py:40
  19.3 266.1 %all-reduce.2.cloned.1.call-start = ((), (), s32[]{:S(2)}) async-start(), calls=%async_computation.2 | async-start | bytes 8388608 | tf_op jit(solution)/shard_map/psum | solution.py:93
  177.4 0.7 copy-start.3
  291.8 5.7 %copy-start = (bf16[64,8192]{1,0:T(8,128)(2,1)S(1)}, bf16[64,8192]{1,0:T(8,128)(2,1)}, u32[]{:S(2)}) copy-start(bf16[64,8192]{1,0:T(8,128)(2,1)} %param.16) | copy-start | bytes 3145732
  297.5 0.8 copy-start.2
Sparse Core Ops, SparseCore 0:
  10.5 63.2 all-gather.1
  177.6 107.8 all-reduce.1
